TPU v7x, 256 devices: a whole 4x4x8 slice. The times are simulated.
256 devices in a mesh: dp: 64 (over z, y, core), mp: 4 (over x).
Axes of the slice: x: 4, y: 4, z: 8, core: 2. Of those that a mesh axis runs over, the one named last changes fastest.
Arguments:
- tree_query: bfloat16 [8192, 2048], P('dp', 'mp'), may hold values from -6 to 6
- new_kv: bfloat16 [8192, 2, 512], P('dp', None, 'mp'), may hold values from -6 to 6
- kv_cache: bfloat16 [2560, 2, 128, 512], P('dp', None, None, 'mp'), may hold values from -4 to 4
- page_table: int32 [128, 32], P('dp'), may hold values from 0 to 39, as said below
- cache_len: int32 [128], P('dp'), may hold values from 2 to 4096, as said below
- tree_mask: int32 [128, 64, 64], P('dp'), may hold values from 0 to 1, as said below
- out_weight: bfloat16 [2048, 2048], P('mp'), may hold values from -0.5 to 0.5
- residual_in: bfloat16 [8192, 2048], P('dp'), may hold values from -3 to 3
- norm_gain: float32 [2048], replicated, may hold values from 0.25 to 1.75
- route_ids: int32 [8192, 6], P('dp'), may hold values from 0 to 63, all different within a row; in each aligned block of 128 rows (0 to 127, 128 to 255, ...) at most 16 rows name the same one
- route_weight: float32 [8192, 6], P('dp'), may hold values from 0.05 to 0.5
- w_gate: bfloat16 [64, 2048, 1408], P('dp', None, 'mp'), may hold values from -0.125 to 0.125
- w_up: bfloat16 [64, 2048, 1408], P('dp', None, 'mp'), may hold values from -0.125 to 0.125
- w_down: bfloat16 [64, 1408, 2048], P('dp', None, 'mp'), may hold values from -0.15625 to 0.15625
- shared_gate: bfloat16 [2048, 2816], P('dp', 'mp'), may hold values from -0.125 to 0.125
- shared_up: bfloat16 [2048, 2816], P('dp', 'mp'), may hold values from -0.125 to 0.125
- shared_down: bfloat16 [2816, 2048], P('mp', 'dp'), may hold values from -0.109375 to 0.109375
Outputs:
- layer_out: bfloat16 [8192, 2048], P('dp', 'mp')
Inputs may be any that keep to these rules, and one draw needn't show every extreme that they name: `route_ids`: each row names 6 different experts. Within the rows of one index of dp (aligned blocks of 128 rows) no expert is named by more than 16 rows, and in some block one expert is named by exactly 16 rows. `cache_len`: the pages of the requests of one index of dp number at most 40 together; some request has exactly 4096 cached positions. `page_table`: entry [r, j] is the slot, in the pool of the index of dp that holds request r, of the page with cache positions j * 128 to j * 128 + 127. Entries with j * 128 < cache_len[r] are distinct over the requests of one index of dp; the other entries are valid slots whose contents are not read. tree_mask[r, i, u] is 1 where tree node u is node i or an ancestor of it, else 0; node 0 is the root and each other node's parent has a smaller index.
All inputs are finite; a program needn't handle non-finite values.
Results may differ from a plain program's by a relative error of at most 0.009.
Values may be sent and summed in bfloat16 or wider, within the bound.
No kernel may reach another device: no remote copies, remote signals or barrier semaphores. Data moves between devices by JAX's collectives and lax.ppermute only.
A program may use at most 128 MiB of HBM per device.

v0:
```python
import jax
import jax.numpy as jnp
from jax import lax
from jax.sharding import PartitionSpec as P

NEGATIVE_FILL = -1e30
EPSILON = 1e-05


def normalize(rows, gain):
    values = rows.astype(jnp.float32)
    mean_square = jnp.mean(values * values, axis=-1, keepdims=True)
    return (values * lax.rsqrt(mean_square + EPSILON) * gain).astype(jnp.bfloat16)


def attend_requests(
    queries, tree_keys, tree_values, tree_allow, kv_cache, page_table, cache_len, score_scale
):

    def per_request(request_item):
        q_rows, own_keys, own_values, allow_rows, table_row, length = request_item
        kv_pages = kv_cache[table_row]
        cache_keys = kv_pages[:, 0].reshape(-1, kv_pages.shape[-1])
        cache_values = kv_pages[:, 1].reshape(-1, kv_pages.shape[-1])
        live_mask = (jnp.arange(cache_keys.shape[0], dtype=jnp.int32) < length)[None, :]
        cache_scores = (
            jnp.einsum("qd,kd->qk", q_rows, cache_keys, preferred_element_type=jnp.float32)
            * score_scale
        )
        cache_scores = jnp.where(live_mask, cache_scores, NEGATIVE_FILL)
        tree_scores = (
            jnp.einsum("qd,ud->qu", q_rows, own_keys, preferred_element_type=jnp.float32)
            * score_scale
        )
        tree_scores = jnp.where(allow_rows, tree_scores, NEGATIVE_FILL)
        row_peak = jnp.maximum(jnp.max(cache_scores, axis=1), jnp.max(tree_scores, axis=1))[:, None]
        cache_probs = jnp.where(live_mask, jnp.exp(cache_scores - row_peak), 0.0)
        tree_probs = jnp.where(allow_rows, jnp.exp(tree_scores - row_peak), 0.0)
        denom_sum = jnp.sum(cache_probs, axis=1) + jnp.sum(tree_probs, axis=1)
        weighted = jnp.dot(
            cache_probs.astype(jnp.bfloat16), cache_values, preferred_element_type=jnp.float32
        )
        weighted = weighted + jnp.dot(
            tree_probs.astype(jnp.bfloat16), own_values, preferred_element_type=jnp.float32
        )
        return (weighted / denom_sum[:, None]).astype(jnp.bfloat16)

    return lax.map(
        per_request, (queries, tree_keys, tree_values, tree_allow, page_table, cache_len)
    )


def gather_mp(block, axis):
    parts = lax.axis_size("mp")
    copies = jnp.broadcast_to(block[None], (parts,) + block.shape)
    pieces = lax.all_to_all(copies, "mp", split_axis=0, concat_axis=0, tiled=True)
    pieces = jnp.moveaxis(pieces, 0, axis)
    shape = list(block.shape)
    shape[axis] = shape[axis] * parts
    return pieces.reshape(shape)


def scatter_sum_mp(terms):
    parts = lax.axis_size("mp")
    rows, width = terms.shape
    blocks = terms.reshape(rows, parts, width // parts).transpose(1, 0, 2)
    pieces = lax.all_to_all(blocks, "mp", split_axis=0, concat_axis=0, tiled=True)
    return jnp.sum(pieces.astype(jnp.float32), axis=0)


def run_experts(rows, w_gate, w_up, w_down):
    source_count, slot_count, model_width = rows.shape
    flat_rows = rows.reshape(source_count * slot_count, model_width)
    gate_proj = jnp.dot(flat_rows, w_gate[0], preferred_element_type=jnp.float32)
    up_proj = jnp.dot(flat_rows, w_up[0], preferred_element_type=jnp.float32)
    hidden_act = (jax.nn.silu(gate_proj) * up_proj).astype(jnp.bfloat16)
    down_rows = w_down[0]
    summed = jnp.dot(gather_mp(hidden_act, 1), down_rows, preferred_element_type=jnp.float32)
    outputs = summed.astype(jnp.bfloat16).reshape(source_count, slot_count, w_down.shape[2])
    return lax.all_to_all(outputs, "dp", split_axis=0, concat_axis=0, tiled=True)


def shared_experts(normed_rows, shared_gate, shared_up, shared_down):
    gate_total = jnp.dot(
        normed_rows,
        lax.all_gather(shared_gate, "dp", axis=0, tiled=True),
        preferred_element_type=jnp.float32,
    )
    up_total = jnp.dot(
        normed_rows,
        lax.all_gather(shared_up, "dp", axis=0, tiled=True),
        preferred_element_type=jnp.float32,
    )
    shared_hidden = (jax.nn.silu(gate_total) * up_total).astype(jnp.bfloat16)
    terms = jnp.dot(
        shared_hidden,
        lax.all_gather(shared_down, "dp", axis=1, tiled=True),
        preferred_element_type=jnp.float32,
    )
    return scatter_sum_mp(terms.astype(jnp.bfloat16))


def on_device(
    tree_query,
    new_kv,
    kv_cache,
    page_table,
    cache_len,
    tree_mask,
    out_weight,
    residual_in,
    norm_gain,
    route_ids,
    route_weight,
    w_gate,
    w_up,
    w_down,
    shared_gate,
    shared_up,
    shared_down,
):
    tok_rows = tree_query.shape[0]
    req_count = cache_len.shape[0]
    tree_len = tree_mask.shape[1]
    head_width = new_kv.shape[2]
    local_heads = tree_query.shape[1] // head_width
    score_scale = head_width ** (-0.5)
    queries = tree_query.reshape(req_count, tree_len, local_heads, head_width)
    queries = queries.transpose(0, 2, 1, 3).reshape(req_count, local_heads * tree_len, head_width)
    tree_keys = new_kv[:, 0, :].reshape(req_count, tree_len, head_width)
    tree_values = new_kv[:, 1, :].reshape(req_count, tree_len, head_width)
    tree_allow = jnp.tile(tree_mask, (1, local_heads, 1)) == 1
    attended = attend_requests(
        queries, tree_keys, tree_values, tree_allow, kv_cache, page_table, cache_len, score_scale
    )
    attended = attended.reshape(req_count, local_heads, tree_len, head_width).transpose(0, 2, 1, 3)
    attended = attended.reshape(tok_rows, local_heads * head_width)
    partial_value = jnp.dot(attended, out_weight, preferred_element_type=jnp.float32)
    model_width = residual_in.shape[1]
    quarter = model_width // lax.axis_size("mp")
    col_start = lax.axis_index("mp") * quarter
    experts = lax.axis_size("dp") * w_gate.shape[0]
    route_count = route_ids.shape[1]
    capacity = min(tok_rows, 4 * tok_rows * route_count // (3 * experts))
    expert_ids = route_ids.reshape(-1)
    onehot = (expert_ids[:, None] == jnp.arange(experts, dtype=jnp.int32)[None, :]).astype(
        jnp.int32
    )
    slot_index = jnp.sum((jnp.cumsum(onehot, axis=0) - onehot) * onehot, axis=1)
    own_residual = lax.dynamic_slice_in_dim(residual_in, col_start, quarter, 1)
    own_stream = (own_residual.astype(jnp.float32) + scatter_sum_mp(partial_value)).astype(
        jnp.bfloat16
    )
    stream = gather_mp(own_stream, 1)
    normed_rows = normalize(stream, norm_gain)
    codes = (expert_ids * capacity + slot_index).reshape(tok_rows, route_count)
    slots = jnp.arange(experts * capacity, dtype=jnp.int32)
    placing = jnp.any(codes[None, :, :] == slots[:, None, None], axis=2).astype(jnp.bfloat16)
    buffer = jnp.dot(placing, normed_rows, preferred_element_type=jnp.float32).astype(jnp.bfloat16)
    buffer = buffer.reshape(experts, capacity, normed_rows.shape[1])
    results = run_experts(
        lax.all_to_all(buffer, "dp", split_axis=0, concat_axis=0, tiled=True), w_gate, w_up, w_down
    )
    shared_out = shared_experts(normed_rows, shared_gate, shared_up, shared_down)
    result_rows = results.reshape(experts * capacity, quarter)
    picked = (
        result_rows[expert_ids * capacity + slot_index]
        .reshape(tok_rows, route_count, quarter)
        .astype(jnp.float32)
    )
    mixture = jnp.einsum("tk,tkc->tc", route_weight, picked, precision=lax.Precision.HIGHEST)
    return (own_stream.astype(jnp.float32) + shared_out.astype(jnp.float32) + mixture).astype(
        jnp.bfloat16
    )


def solution(mesh):
    return jax.shard_map(
        on_device,
        mesh=mesh,
        in_specs=(
            P("dp", "mp"),
            P("dp", None, "mp"),
            P("dp", None, None, "mp"),
            P("dp", None),
            P("dp"),
            P("dp", None, None),
            P("mp", None),
            P("dp", None),
            P(),
            P("dp", None),
            P("dp", None),
            P("dp", None, "mp"),
            P("dp", None, "mp"),
            P("dp", None, "mp"),
            P("dp", "mp"),
            P("dp", "mp"),
            P("mp", "dp"),
        ),
        out_specs=P("dp", "mp"),
        check_vma=False,
    )
```

profile of v0, /device:TPU:1, one launch (start us, length us, event | category | flops | bytes accessed | tf_op | source)
XLA Modules:
  0.0 334.9 jit_solution(15534831628222421942)
XLA Ops:
  13.0 18.3 %while.10 = (s32[]{:T(128)}, bf16[2,256,128]{2,1,0:T(8,128)(2,1)}, s32[2]{0:T(128)}, bf16[2,256,128]{2,1,0:T(8,128)(2,1)}, s32[2,32]{1,0:T(2,128)}, /*index=5*/b...) while((s32[]{:T(128)}, bf16[2,256,128]{2,1,0:T(8,128)(2,1)}, ...), condition=%wide.region_5.6_spmd, body=%wide.region_0.5_spmd.sunk | while | flops 554947200 | bytes 25811812 | solution.py:48
  13.7 2.7 gather_fusion
  22.8 2.7 gather_fusion
  33.0 2.9 copy.62
  35.8 2.7 convolution_bitcast_fusion
  38.6 4.8 %all-to-all-start = ((f32[4,128,512]{2,1,0:T(8,128)}), f32[4,128,512]{2,1,0:T(8,128)S(1)}, u32[]{:S(2)}, u32[]{:S(2)}) async-start(f32[4,128,512]{2,1,0:T(8,128)} %convolution_bitcast_fusion), calls=%async_computation | async-start | bytes 2097152 | tf_op jit(solution)/shard_map/all_to_all | solution.py:67
  46.7 9.9 %all-to-all-done = f32[4,128,512]{2,1,0:T(8,128)S(1)} async-done(((f32[4,128,512]{2,1,0:T(8,128)}), f32[4,128,512]{2,1,0:T(8,128)S(1)}, u32[]{:S(2)}, u32[]{:S(2)}) %all-to-all-start) | async-done | bytes 1048608 | tf_op jit(solution)/shard_map/all_to_all | solution.py:67
  58.6 3.5 %all-to-all-start.1 = ((bf16[4,128,512]{1,2,0:T(8,128)(2,1)}), bf16[4,128,512]{1,2,0:T(8,128)(2,1)S(1)}, u32[]{:S(2)}, u32[]{:S(2)}) async-start(bf16[4,128,512]{1,2,0:T(8,128)(2,1)} %broadcast_in_dim.54), calls=%async_computation.1 | async-start | bytes 1048576 | tf_op jit(solution)/shard_map/all_to_all | solution.py:56
  63.0 6.0 %all-to-all-done.1 = bf16[4,128,512]{1,2,0:T(8,128)(2,1)S(1)} async-done(((bf16[4,128,512]{1,2,0:T(8,128)(2,1)}), bf16[4,128,512]{1,2,0:T(8,128)(2,1)S(1)}, u32[]{:S(2)}, u32[]{:S(2)}) %all-to-all-start.1) | async-done | bytes 524320 | tf_op jit(solution)/shard_map/all_to_all | solution.py:56
  69.6 3.2 convolution_convert_fusion
  72.9 16.3 %all-to-all-start.3 = ((bf16[64,16,2048]{2,1,0:T(8,128)(2,1)}), bf16[64,16,2048]{2,1,0:T(8,128)(2,1)}, u32[]{:S(2)}, u32[]{:S(2)}) async-start(bf16[64,16,2048]{2,1,0:T(8,128)(2,1)} %bitcast.159), calls=%async_computation.3 | async-start | bytes 8388608 | tf_op jit(solution)/shard_map/all_to_all | solution.py:162
  89.9 102.8 %all-to-all-done.3 = bf16[64,16,2048]{2,1,0:T(8,128)(2,1)} async-done(((bf16[64,16,2048]{2,1,0:T(8,128)(2,1)}), bf16[64,16,2048]{2,1,0:T(8,128)(2,1)}, u32[]{:S(2)}, u32[]{:S(2)}) %all-to-all-start.3) | async-done | bytes 4194336 | tf_op jit(solution)/shard_map/all_to_all | solution.py:162
  192.7 4.4 %fusion.36 = f32[1024,352]{0,1:T(8,128)S(1)} fusion(bf16[1024,2048]{1,0:T(8,128)(2,1)} %bitcast.24, bf16[1,2048,352]{1,2,0:T(8,128)(2,1)} %param.30), kind=kOutput, calls=%fused_computation.50 | convolution fusion | flops 1476395008 | bytes 7077888 | tf_op jit(solution)/shard_map/dot_general | solution.py:74
  197.1 4.0 %fusion.38 = bf16[1024,352]{0,1:T(8,128)(2,1)S(1)} fusion(bf16[1024,2048]{1,0:T(8,128)(2,1)} %bitcast.24, bf16[1,2048,352]{1,2,0:T(8,128)(2,1)S(1)} %copy-done.10, f32[1024,352]{0,1:T(8,128)S(1)} %fusion.36), kind=kOutput, calls=%fused_computation.52 | convolution fusion | flops 1478557696 | bytes 7798784 | tf_op jit(solution)/shard_map/dot_general | solution.py:75
  203.2 4.6 %all-to-all-start.4 = ((bf16[4,1024,352]{1,2,0:T(8,128)(2,1)}), bf16[4,1024,352]{1,2,0:T(8,128)(2,1)}, u32[]{:S(2)}, u32[]{:S(2)}) async-start(bf16[4,1024,352]{1,2,0:T(8,128)(2,1)} %broadcast_in_dim.55), calls=%async_computation.4 | async-start | bytes 5767168 | tf_op jit(solution)/shard_map/all_to_all | solution.py:56
  207.8 3.2 fusion.62
  211.0 56.2 %all-gather.8.cloned.1.call-done = bf16[704,2048]{0,1:T(8,128)(2,1)} async-done(((bf16[704,32]{0,1:T(8,128)(2,1)}), bf16[704,2048]{0,1:T(8,128)(2,1)}) %all-gather.8.cloned.1.call-update) | async-done | bytes 2883600 | tf_op jit(solution)/shard_map/all_gather | solution.py:97
  267.2 6.2 %convolution_convert_fusion.1 = bf16[128,2048]{1,0:T(8,128)(2,1)S(1)} fusion(bf16[704,2048]{0,1:T(8,128)(2,1)} %all-gather.8.cloned.1.call-done, bf16[128,2048]{0,1:T(8,128)(2,1)S(1)} %fusion.43, bf16[2048,704]{1,0:T(8,128)(2,1)} %all-gather.6.cloned.1.call-done, f32[128,704]{0,1:T(8,128)S(1)} %fusion.62), kind=kOutput, calls=%fused_computation.45 | convolution fusion | flops 739000320 | bytes 7176192 | tf_op jit(solution)/shard_map/dot_general | solution.py:95
  274.2 4.0 %all-to-all-start.2 = ((bf16[4,128,512]{2,1,0:T(8,128)(2,1)}), bf16[4,128,512]{2,1,0:T(8,128)(2,1)S(1)}, u32[]{:S(2)}, u32[]{:S(2)}) async-start(bf16[4,128,512]{2,1,0:T(8,128)(2,1)} %bitcast.126), calls=%async_computation.2 | async-start | bytes 1048576 | tf_op jit(solution)/shard_map/all_to_all | solution.py:67
  278.2 4.6 %convolution_convert_fusion.2 = bf16[1024,512]{1,0:T(8,128)(2,1)} fusion(bf16[1024,1408]{0,1:T(8,128)(2,1)} %bitcast.28, bf16[1,1408,512]{2,1,0:T(8,128)(2,1)S(1)} %copy-done), kind=kOutput, calls=%fused_computation.46 | convolution fusion | flops 1476919296 | bytes 5373952 | tf_op jit(solution)/shard_map/dot_general | solution.py:78
  282.8 4.4 %all-to-all-done.2 = bf16[4,128,512]{2,1,0:T(8,128)(2,1)S(1)} async-done(((bf16[4,128,512]{2,1,0:T(8,128)(2,1)}), bf16[4,128,512]{2,1,0:T(8,128)(2,1)S(1)}, u32[]{:S(2)}, u32[]{:S(2)}) %all-to-all-start.2) | async-done | bytes 524320 | tf_op jit(solution)/shard_map/all_to_all | solution.py:67
  287.2 7.6 %all-to-all-start.5 = ((bf16[64,16,512]{2,1,0:T(8,128)(2,1)}), bf16[64,16,512]{2,1,0:T(8,128)(2,1)S(1)}, u32[]{:S(2)}, u32[]{:S(2)}) async-start(bf16[64,16,512]{2,1,0:T(8,128)(2,1)} %bitcast.163), calls=%async_computation.5 | async-start | bytes 2097152 | tf_op jit(solution)/shard_map/all_to_all | solution.py:80
  295.9 26.9 %all-to-all-done.5 = bf16[64,16,512]{2,1,0:T(8,128)(2,1)S(1)} async-done(((bf16[64,16,512]{2,1,0:T(8,128)(2,1)}), bf16[64,16,512]{2,1,0:T(8,128)(2,1)S(1)}, u32[]{:S(2)}, u32[]{:S(2)}) %all-to-all-start.5) | async-done | bytes 1048608 | tf_op jit(solution)/shard_map/all_to_all | solution.py:80
  322.8 2.7 gather_fusion.1
  (114 shorter events, 35.0 us)
Async XLA Ops:
  6.5 271.7 %copy-start = (bf16[1,1408,512]{2,1,0:T(8,128)(2,1)S(1)}, bf16[1,1408,512]{2,1,0:T(8,128)(2,1)}, u32[]{:S(2)}) copy-start(bf16[1,1408,512]{2,1,0:T(8,128)(2,1)} %param.32) | copy-start | bytes 4325380
  6.5 201.2 %all-gather.4.cloned.1.call-start = ((), (), s32[]{:S(2)}) async-start(), calls=%async_computation.6 | async-start | bytes 3194880 | tf_op jit(solution)/shard_map/all_gather | solution.py:86
  16.4 1.9 copy-start.1
  16.6 2.6 copy-start.2
  16.6 2.6 copy-start.3
  20.2 1.0 copy-start.4
  20.3 1.0 copy-start.6
  25.5 1.9 copy-start.1
  25.7 2.6 copy-start.2
  25.7 2.6 copy-start.3
  29.4 1.0 copy-start.4
  29.4 1.0 copy-start.6
  35.8 8.3 %copy-start.8 = (s32[128,6]{0,1:T(8,128)S(1)}, s32[128,6]{0,1:T(8,128)}, u32[]{:S(2)}) copy-start(s32[128,6]{0,1:T(8,128)} %param.28) | copy-start | bytes 9220
  38.6 18.1 %all-to-all-start = ((f32[4,128,512]{2,1,0:T(8,128)}), f32[4,128,512]{2,1,0:T(8,128)S(1)}, u32[]{:S(2)}, u32[]{:S(2)}) async-start(f32[4,128,512]{2,1,0:T(8,128)} %convolution_bitcast_fusion), calls=%async_computation | async-start | bytes 2097152 | tf_op jit(solution)/shard_map/all_to_all | solution.py:67
  43.4 25.9 %copy-start.7 = (f32[2048]{0:T(1024)S(1)}, f32[2048]{0:T(1024)}, u32[]{:S(2)}) copy-start(f32[2048]{0:T(1024)} %param.27) | copy-start | bytes 24580
  43.4 167.6 %all-gather.6.cloned.1.call-start = ((), (), s32[]{:S(2)}) async-start(), calls=%async_computation.7 | async-start | bytes 3194880 | tf_op jit(solution)/shard_map/all_gather | solution.py:91
  58.6 10.4 %all-to-all-start.1 = ((bf16[4,128,512]{1,2,0:T(8,128)(2,1)}), bf16[4,128,512]{1,2,0:T(8,128)(2,1)S(1)}, u32[]{:S(2)}, u32[]{:S(2)}) async-start(bf16[4,128,512]{1,2,0:T(8,128)(2,1)} %broadcast_in_dim.54), calls=%async_computation.1 | async-start | bytes 1048576 | tf_op jit(solution)/shard_map/all_to_all | solution.py:56
  72.9 119.8 %all-to-all-start.3 = ((bf16[64,16,2048]{2,1,0:T(8,128)(2,1)}), bf16[64,16,2048]{2,1,0:T(8,128)(2,1)}, u32[]{:S(2)}, u32[]{:S(2)}) async-start(bf16[64,16,2048]{2,1,0:T(8,128)(2,1)} %bitcast.159), calls=%async_computation.3 | async-start | bytes 8388608 | tf_op jit(solution)/shard_map/all_to_all | solution.py:162
  89.2 178.0 %all-gather.8.cloned.1.call-start = ((), (), s32[]{:S(2)}) async-start(), calls=%async_computation.8 | async-start | bytes 3194880 | tf_op jit(solution)/shard_map/all_gather | solution.py:97
  192.7 4.4 %copy-start.10 = (bf16[1,2048,352]{1,2,0:T(8,128)(2,1)S(1)}, bf16[1,2048,352]{1,2,0:T(8,128)(2,1)}, u32[]{:S(2)}) copy-start(bf16[1,2048,352]{1,2,0:T(8,128)(2,1)} %param.31) | copy-start | bytes 4325380
  203.2 71.1 %all-to-all-start.4 = ((bf16[4,1024,352]{1,2,0:T(8,128)(2,1)}), bf16[4,1024,352]{1,2,0:T(8,128)(2,1)}, u32[]{:S(2)}, u32[]{:S(2)}) async-start(bf16[4,1024,352]{1,2,0:T(8,128)(2,1)} %broadcast_in_dim.55), calls=%async_computation.4 | async-start | bytes 5767168 | tf_op jit(solution)/shard_map/all_to_all | solution.py:56
  274.2 13.0 %all-to-all-start.2 = ((bf16[4,128,512]{2,1,0:T(8,128)(2,1)}), bf16[4,128,512]{2,1,0:T(8,128)(2,1)S(1)}, u32[]{:S(2)}, u32[]{:S(2)}) async-start(bf16[4,128,512]{2,1,0:T(8,128)(2,1)} %bitcast.126), calls=%async_computation.2 | async-start | bytes 1048576 | tf_op jit(solution)/shard_map/all_to_all | solution.py:67
  278.2 16.8 %copy-start.9 = (f32[128,6]{0,1:T(8,128)S(1)}, f32[128,6]{0,1:T(8,128)}, u32[]{:S(2)}) copy-start(f32[128,6]{0,1:T(8,128)} %param.29) | copy-start | bytes 9220
  287.2 35.6 %all-to-all-start.5 = ((bf16[64,16,512]{2,1,0:T(8,128)(2,1)}), bf16[64,16,512]{2,1,0:T(8,128)(2,1)S(1)}, u32[]{:S(2)}, u32[]{:S(2)}) async-start(bf16[64,16,512]{2,1,0:T(8,128)(2,1)} %bitcast.163), calls=%async_computation.5 | async-start | bytes 2097152 | tf_op jit(solution)/shard_map/all_to_all | solution.py:80
  (4 other events, 2.6 us)
Sparse Core Ops, SparseCore 0:
  10.1 82.5 all-gather.3
  95.5 89.2 all-gather.5
  187.6 79.5 all-gather.7
where the time goes:
time: 336 us; the launch traced here: 335 us
  waiting for transfers between devices  208 us (62%)
  starting transfers between devices  41 us (12%)
  matrix products  33.6 us (10%)
  local copies, waits for them, and re-layouts  26.5 us (8%)
  between operations  13.4 us (4%)
  other arithmetic  12 us (4%)
    all_to_all x1, waiting for transfers between devices, on_device(): lax.all_to_all(buffer, 'dp', split_axis=0, concat_axis=0, tiled=True)  103 us
    all_gather x1, waiting for transfers between devices, shared_experts(): lax.all_gather(shared_down, 'dp', axis=1, tiled=True)  56.2 us
    all_to_all x1, waiting for transfers between devices, run_experts(): lax.all_to_all(outputs, 'dp', split_axis=0, concat_axis=0, tiled=True)  26.9 us
    all_to_all x1, starting transfers between devices, on_device(): lax.all_to_all(buffer, 'dp', split_axis=0, concat_axis=0, tiled=True)  16.3 us
    all_to_all x2, waiting for transfers between devices, scatter_sum_mp(): lax.all_to_all(blocks, 'mp', split_axis=0, concat_axis=0, tiled=True)  14.4 us
    all_to_all x2, starting transfers between devices, scatter_sum_mp(): lax.all_to_all(blocks, 'mp', split_axis=0, concat_axis=0, tiled=True)  8.82 us
    all_to_all x2, starting transfers between devices, gather_mp(): lax.all_to_all(copies, 'mp', split_axis=0, concat_axis=0, tiled=True)  8.07 us
    all_to_all x1, starting transfers between devices, run_experts(): lax.all_to_all(outputs, 'dp', split_axis=0, concat_axis=0, tiled=True)  7.56 us
  transfers between devices with their start and end apart: 9, of which 6 were waited for; matrix products, arithmetic and copies ran while one was open for 19% of the time, Pallas kernels for 0%

commit v1 on v0

--- a/solution.py
+++ b/solution.py
@@ -92,11 +92,13 @@
         preferred_element_type=jnp.float32,
     )
     shared_hidden = (jax.nn.silu(gate_total) * up_total).astype(jnp.bfloat16)
-    terms = jnp.dot(
-        shared_hidden,
-        lax.all_gather(shared_down, "dp", axis=1, tiled=True),
-        preferred_element_type=jnp.float32,
-    )
+
+    def matrix_fit(z):
+        y_new = tuple((z for _ in range(jax.lax.axis_size("dp"))))
+        later = jnp.stack(y_new)
+        return jnp.concatenate(jax.lax.all_to_all(later, "dp", 0, 0), 1)
+
+    terms = jnp.dot(shared_hidden, matrix_fit(shared_down), preferred_element_type=jnp.float32)
     return scatter_sum_mp(terms.astype(jnp.bfloat16))
 
 

time: 336 us -> 383 us (1.14)
  waiting for transfers between devices: 208 us -> 242 us
  starting transfers between devices: 41 us -> 51.5 us
    all_to_all x0 -> x1, waiting for transfers between devices: none -> 68.5 us  [matrix_fit(): return jnp.concatenate(jax.lax.all_to_all(later, 'dp', 0, 0), 1)]
    all_gather x1 -> x0, waiting for transfers between devices: 56.2 us -> none  [shared_experts(): lax.all_gather(shared_down, 'dp', axis=1, tiled=True)]
    all_to_all x2, waiting for transfers between devices: 6.02 us -> 26.3 us  [gather_mp(): lax.all_to_all(copies, 'mp', split_axis=0, concat_axis=0, tiled=True)]
    all_to_all x0 -> x1, starting transfers between devices: none -> 7.34 us  [matrix_fit(): return jnp.concatenate(jax.lax.all_to_all(later, 'dp', 0, 0), 1)]
  transfers between devices with their start and end apart: 9 -> 9, of which waited for: 6 -> 8; matrix products, arithmetic and copies ran while one was open for 19% -> 8% of each run, Pallas kernels for 0% -> 0%
where the time goes in v1:
time: 383 us; the launch traced here: 381 us
  waiting for transfers between devices  242 us (63%)
  starting transfers between devices  51.5 us (13%)
  matrix products  33.6 us (9%)
  local copies, waits for them, and re-layouts  28.5 us (7%)
  between operations  13.7 us (4%)
  other arithmetic  12 us (3%)
    all_to_all x1, waiting for transfers between devices, on_device(): lax.all_to_all(buffer, 'dp', split_axis=0, concat_axis=0, tiled=True)  103 us
    all_to_all x1, waiting for transfers between devices, matrix_fit(): return jnp.concatenate(jax.lax.all_to_all(later, 'dp', 0, 0), 1)  68.5 us
    all_to_all x1, waiting for transfers between devices, run_experts(): lax.all_to_all(outputs, 'dp', split_axis=0, concat_axis=0, tiled=True)  26.9 us
    all_to_all x2, waiting for transfers between devices, gather_mp(): lax.all_to_all(copies, 'mp', split_axis=0, concat_axis=0, tiled=True)  26.3 us
    all_to_all x1, starting transfers between devices, on_device(): lax.all_to_all(buffer, 'dp', split_axis=0, concat_axis=0, tiled=True)  16.4 us
    all_to_all x2, waiting for transfers between devices, scatter_sum_mp(): lax.all_to_all(blocks, 'mp', split_axis=0, concat_axis=0, tiled=True)  13 us
    all_to_all x1, starting transfers between devices, run_experts(): lax.all_to_all(outputs, 'dp', split_axis=0, concat_axis=0, tiled=True)  11.2 us
    all_to_all x2, starting transfers between devices, scatter_sum_mp(): lax.all_to_all(blocks, 'mp', split_axis=0, concat_axis=0, tiled=True)  8.31 us
  transfers between devices with their start and end apart: 9, of which 8 were waited for; matrix products, arithmetic and copies ran while one was open for 8% of the time, Pallas kernels for 0%

profile of v1, /device:TPU:1, one launch (start us, length us, event | category | flops | bytes accessed | tf_op | source)
XLA Modules:
  0.0 381.4 jit_solution(15175374437302636974)
XLA Ops:
  12.3 18.3 %while.10 = (s32[]{:T(128)}, bf16[2,256,128]{2,1,0:T(8,128)(2,1)}, s32[2]{0:T(128)}, bf16[2,256,128]{2,1,0:T(8,128)(2,1)}, s32[2,32]{1,0:T(2,128)}, /*index=5*/b...) while((s32[]{:T(128)}, bf16[2,256,128]{2,1,0:T(8,128)(2,1)}, ...), condition=%wide.region_5.6_spmd, body=%wide.region_0.5_spmd.sunk | while | flops 554947200 | bytes 25811812 | solution.py:48
  13.0 2.7 gather_fusion
  32.3 2.9 copy.63
  35.2 2.7 convolution_bitcast_fusion
  37.9 4.8 %all-to-all-start = ((f32[4,128,512]{2,1,0:T(8,128)}), f32[4,128,512]{2,1,0:T(8,128)S(1)}, u32[]{:S(2)}, u32[]{:S(2)}) async-start(f32[4,128,512]{2,1,0:T(8,128)} %convolution_bitcast_fusion), calls=%async_computation | async-start | bytes 2097152 | tf_op jit(solution)/shard_map/all_to_all | solution.py:67
  45.3 10.7 %all-to-all-done = f32[4,128,512]{2,1,0:T(8,128)S(1)} async-done(((f32[4,128,512]{2,1,0:T(8,128)}), f32[4,128,512]{2,1,0:T(8,128)S(1)}, u32[]{:S(2)}, u32[]{:S(2)}) %all-to-all-start) | async-done | bytes 1048608 | tf_op jit(solution)/shard_map/all_to_all | solution.py:67
  58.0 3.5 all-to-all-start.1
  62.3 6.0 %all-to-all-done.1 = bf16[4,128,512]{1,2,0:T(8,128)(2,1)S(1)} async-done(((bf16[4,128,512]{1,2,0:T(8,128)(2,1)}), bf16[4,128,512]{1,2,0:T(8,128)(2,1)S(1)}, u32[]{:S(2)}, u32[]{:S(2)}) %all-to-all-start.1) | async-done | bytes 524320 | tf_op jit(solution)/shard_map/all_to_all | solution.py:56
  69.0 3.3 convolution_convert_fusion
  72.3 16.4 %all-to-all-start.4 = ((bf16[64,16,2048]{2,1,0:T(8,128)(2,1)}), bf16[64,16,2048]{2,1,0:T(8,128)(2,1)}, u32[]{:S(2)}, u32[]{:S(2)}) async-start(bf16[64,16,2048]{2,1,0:T(8,128)(2,1)} %bitcast.162), calls=%async_computation.4 | async-start | bytes 8388608 | tf_op jit(solution)/shard_map/all_to_all | solution.py:164
  89.4 102.9 %all-to-all-done.4 = bf16[64,16,2048]{2,1,0:T(8,128)(2,1)} async-done(((bf16[64,16,2048]{2,1,0:T(8,128)(2,1)}), bf16[64,16,2048]{2,1,0:T(8,128)(2,1)}, u32[]{:S(2)}, u32[]{:S(2)}) %all-to-all-start.4) | async-done | bytes 4194336 | tf_op jit(solution)/shard_map/all_to_all | solution.py:164
  194.3 7.3 %all-to-all-start.2 = ((bf16[64,704,32]{1,2,0:T(8,128)(2,1)}), bf16[64,704,32]{1,2,0:T(8,128)(2,1)}, u32[]{:S(2)}, u32[]{:S(2)}) async-start(bf16[64,704,32]{1,2,0:T(8,128)(2,1)} %stack.2), calls=%async_computation.2 | async-start | bytes 6291456 | tf_op jit(solution)/shard_map/all_to_all | solution.py:99
  202.4 4.4 %fusion.36 = f32[1024,352]{0,1:T(8,128)S(1)} fusion(bf16[1024,2048]{1,0:T(8,128)(2,1)} %bitcast.26, bf16[1,2048,352]{1,2,0:T(8,128)(2,1)} %param.30), kind=kOutput, calls=%fused_computation.50 | convolution fusion | flops 1476395008 | bytes 7077888 | tf_op jit(solution)/shard_map/dot_general | solution.py:74
  206.8 4.0 %fusion.38 = bf16[1024,352]{0,1:T(8,128)(2,1)S(1)} fusion(bf16[1024,2048]{1,0:T(8,128)(2,1)} %bitcast.26, bf16[1,2048,352]{1,2,0:T(8,128)(2,1)S(1)} %copy-done.11, f32[1024,352]{0,1:T(8,128)S(1)} %fusion.36), kind=kOutput, calls=%fused_computation.52 | convolution fusion | flops 1478557696 | bytes 7798784 | tf_op jit(solution)/shard_map/dot_general | solution.py:75
  210.9 68.5 %all-to-all-done.2 = bf16[64,704,32]{1,2,0:T(8,128)(2,1)} async-done(((bf16[64,704,32]{1,2,0:T(8,128)(2,1)}), bf16[64,704,32]{1,2,0:T(8,128)(2,1)}, u32[]{:S(2)}, u32[]{:S(2)}) %all-to-all-start.2) | async-done | bytes 2883616 | tf_op jit(solution)/shard_map/all_to_all | solution.py:99
  281.3 4.6 %all-to-all-start.5 = ((bf16[4,1024,352]{1,2,0:T(8,128)(2,1)}), bf16[4,1024,352]{1,2,0:T(8,128)(2,1)}, u32[]{:S(2)}, u32[]{:S(2)}) async-start(bf16[4,1024,352]{1,2,0:T(8,128)(2,1)} %broadcast_in_dim.55), calls=%async_computation.5 | async-start | bytes 5767168 | tf_op jit(solution)/shard_map/all_to_all | solution.py:56
  285.9 3.2 fusion.62
  289.2 2.9 all-gather.5.cloned.1.call-done
  292.0 6.2 %convolution_convert_fusion.1 = bf16[128,2048]{1,0:T(8,128)(2,1)S(1)} fusion(bf16[704,2048]{0,1:T(8,128)(2,1)} %bitcast.22, bf16[128,2048]{0,1:T(8,128)(2,1)S(1)} %fusion.43, bf16[2048,704]{1,0:T(8,128)(2,1)} %all-gather.5.cloned.1.call-done, f32[128,704]{0,1:T(8,128)S(1)} %fusion.62), kind=kOutput, calls=%fused_computation.45 | convolution fusion | flops 739000320 | bytes 7176192 | tf_op jit(solution)/shard_map/dot_general | solution.py:101
  299.1 20.3 %all-to-all-done.5 = bf16[4,1024,352]{1,2,0:T(8,128)(2,1)} async-done(((bf16[4,1024,352]{1,2,0:T(8,128)(2,1)}), bf16[4,1024,352]{1,2,0:T(8,128)(2,1)}, u32[]{:S(2)}, u32[]{:S(2)}) %all-to-all-start.5) | async-done | bytes 2883616 | tf_op jit(solution)/shard_map/all_to_all | solution.py:56
  319.4 3.5 all-to-all-start.3
  322.9 4.6 %convolution_convert_fusion.2 = bf16[1024,512]{1,0:T(8,128)(2,1)} fusion(bf16[1024,1408]{0,1:T(8,128)(2,1)} %bitcast.30, bf16[1,1408,512]{2,1,0:T(8,128)(2,1)S(1)} %copy-done), kind=kOutput, calls=%fused_computation.46 | convolution fusion | flops 1476919296 | bytes 5373952 | tf_op jit(solution)/shard_map/dot_general | solution.py:78
  329.8 11.2 %all-to-all-start.6 = ((bf16[64,16,512]{2,1,0:T(8,128)(2,1)}), bf16[64,16,512]{2,1,0:T(8,128)(2,1)S(1)}, u32[]{:S(2)}, u32[]{:S(2)}) async-start(bf16[64,16,512]{2,1,0:T(8,128)(2,1)} %bitcast.166), calls=%async_computation.6 | async-start | bytes 2097152 | tf_op jit(solution)/shard_map/all_to_all | solution.py:80
  342.0 26.9 %all-to-all-done.6 = bf16[64,16,512]{2,1,0:T(8,128)(2,1)S(1)} async-done(((bf16[64,16,512]{2,1,0:T(8,128)(2,1)}), bf16[64,16,512]{2,1,0:T(8,128)(2,1)S(1)}, u32[]{:S(2)}, u32[]{:S(2)}) %all-to-all-start.6) | async-done | bytes 1048608 | tf_op jit(solution)/shard_map/all_to_all | solution.py:80
  (116 shorter events, 44.0 us)
Async XLA Ops:
  6.5 316.3 %copy-start = (bf16[1,1408,512]{2,1,0:T(8,128)(2,1)S(1)}, bf16[1,1408,512]{2,1,0:T(8,128)(2,1)}, u32[]{:S(2)}) copy-start(bf16[1,1408,512]{2,1,0:T(8,128)(2,1)} %param.32) | copy-start | bytes 4325380
  15.7 1.9 copy-start.1
  15.9 2.6 copy-start.2
  15.9 2.6 copy-start.3
  19.6 1.0 copy-start.4
  19.6 1.0 copy-start.7
  24.8 1.9 copy-start.1
  25.0 2.6 copy-start.2
  25.0 2.6 copy-start.3
  28.7 1.0 copy-start.7
  35.2 7.6 %copy-start.9 = (s32[128,6]{0,1:T(8,128)S(1)}, s32[128,6]{0,1:T(8,128)}, u32[]{:S(2)}) copy-start(s32[128,6]{0,1:T(8,128)} %param.28) | copy-start | bytes 9220
  37.9 18.1 %all-to-all-start = ((f32[4,128,512]{2,1,0:T(8,128)}), f32[4,128,512]{2,1,0:T(8,128)S(1)}, u32[]{:S(2)}, u32[]{:S(2)}) async-start(f32[4,128,512]{2,1,0:T(8,128)} %convolution_bitcast_fusion), calls=%async_computation | async-start | bytes 2097152 | tf_op jit(solution)/shard_map/all_to_all | solution.py:67
  42.7 25.9 %copy-start.8 = (f32[2048]{0:T(1024)S(1)}, f32[2048]{0:T(1024)}, u32[]{:S(2)}) copy-start(f32[2048]{0:T(1024)} %param.27) | copy-start | bytes 24580
  58.0 10.4 %all-to-all-start.1 = ((bf16[4,128,512]{1,2,0:T(8,128)(2,1)}), bf16[4,128,512]{1,2,0:T(8,128)(2,1)S(1)}, u32[]{:S(2)}, u32[]{:S(2)}) async-start(bf16[4,128,512]{1,2,0:T(8,128)(2,1)} %broadcast_in_dim.54), calls=%async_computation.1 | async-start | bytes 1048576 | tf_op jit(solution)/shard_map/all_to_all | solution.py:56
  72.3 120.0 %copy-start.6 = (bf16[704,32]{0,1:T(8,128)(2,1)S(1)}, bf16[704,32]{0,1:T(8,128)(2,1)}, u32[]{:S(2)}) copy-start(bf16[704,32]{0,1:T(8,128)(2,1)} %param.35) | copy-start | bytes 135172
  72.3 120.0 %all-to-all-start.4 = ((bf16[64,16,2048]{2,1,0:T(8,128)(2,1)}), bf16[64,16,2048]{2,1,0:T(8,128)(2,1)}, u32[]{:S(2)}, u32[]{:S(2)}) async-start(bf16[64,16,2048]{2,1,0:T(8,128)(2,1)} %bitcast.162), calls=%async_computation.4 | async-start | bytes 8388608 | tf_op jit(solution)/shard_map/all_to_all | solution.py:164
  88.7 197.3 %all-gather.3.cloned.1.call-start = ((), (), s32[]{:S(2)}) async-start(), calls=%async_computation.7 | async-start | bytes 3194880 | tf_op jit(solution)/shard_map/all_gather | solution.py:86
  194.3 85.0 %all-to-all-start.2 = ((bf16[64,704,32]{1,2,0:T(8,128)(2,1)}), bf16[64,704,32]{1,2,0:T(8,128)(2,1)}, u32[]{:S(2)}, u32[]{:S(2)}) async-start(bf16[64,704,32]{1,2,0:T(8,128)(2,1)} %stack.2), calls=%async_computation.2 | async-start | bytes 6291456 | tf_op jit(solution)/shard_map/all_to_all | solution.py:99
  201.6 90.4 %all-gather.5.cloned.1.call-start = ((), (), s32[]{:S(2)}) async-start(), calls=%async_computation.8 | async-start | bytes 3194880 | tf_op jit(solution)/shard_map/all_gather | solution.py:91
  202.4 4.4 %copy-start.11 = (bf16[1,2048,352]{1,2,0:T(8,128)(2,1)S(1)}, bf16[1,2048,352]{1,2,0:T(8,128)(2,1)}, u32[]{:S(2)}) copy-start(bf16[1,2048,352]{1,2,0:T(8,128)(2,1)} %param.31) | copy-start | bytes 4325380
  281.3 38.1 %all-to-all-start.5 = ((bf16[4,1024,352]{1,2,0:T(8,128)(2,1)}), bf16[4,1024,352]{1,2,0:T(8,128)(2,1)}, u32[]{:S(2)}, u32[]{:S(2)}) async-start(bf16[4,1024,352]{1,2,0:T(8,128)(2,1)} %broadcast_in_dim.55), calls=%async_computation.5 | async-start | bytes 5767168 | tf_op jit(solution)/shard_map/all_to_all | solution.py:56
  319.4 10.4 %all-to-all-start.3 = ((bf16[4,128,512]{2,1,0:T(8,128)(2,1)}), bf16[4,128,512]{2,1,0:T(8,128)(2,1)S(1)}, u32[]{:S(2)}, u32[]{:S(2)}) async-start(bf16[4,128,512]{2,1,0:T(8,128)(2,1)} %bitcast.129), calls=%async_computation.3 | async-start | bytes 1048576 | tf_op jit(solution)/shard_map/all_to_all | solution.py:67
  322.9 18.2 %copy-start.10 = (f32[128,6]{0,1:T(8,128)S(1)}, f32[128,6]{0,1:T(8,128)}, u32[]{:S(2)}) copy-start(f32[128,6]{0,1:T(8,128)} %param.29) | copy-start | bytes 9220
  329.8 39.2 %all-to-all-start.6 = ((bf16[64,16,512]{2,1,0:T(8,128)(2,1)}), bf16[64,16,512]{2,1,0:T(8,128)(2,1)S(1)}, u32[]{:S(2)}, u32[]{:S(2)}) async-start(bf16[64,16,512]{2,1,0:T(8,128)(2,1)} %bitcast.166), calls=%async_computation.6 | async-start | bytes 2097152 | tf_op jit(solution)/shard_map/all_to_all | solution.py:80
  (5 other events, 3.6 us)
Sparse Core Ops, SparseCore 0:
  92.3 90.1 all-gather.2
  205.2 86.7 all-gather.4
